TPU v7x, 256 devices: a whole 4x4x8 slice. The times are simulated.
256 devices in a mesh: chan: 64 (over z, x, core), tm: 4 (over y).
Axes of the slice: x: 4, y: 4, z: 8, core: 2. Of those that a mesh axis runs over, the one named last changes fastest.
Arguments:
- voltages: bfloat16 [2, 2, 64, 2048, 2048], P(None, None, None, 'chan', 'tm'), may hold values from -6 to 6
- weights: bfloat16 [64, 2, 2, 32, 2048], P('chan'), may hold values from -0.09375 to 0.09375
- channel_map: int32 [64], replicated, may hold values from 0 to 63, each once
- sweep_response_taps: float32 [64, 2, 32, 256], P('chan', None, 'tm'), may hold values from -6 to 6
- chirp_length: int32 [32], P('tm'), may hold values from 32 to 256, as said below
Outputs:
- dedispersed: float32 [64, 2, 2, 32, 2048], P('chan', None, None, 'tm')
Inputs may be any that keep to these rules, and one draw needn't show every extreme that they name: `channel_map`: each channel appears once. `chirp_length`: one beam has the longest chirp of exactly 256 samples.
All inputs are finite; a program needn't handle non-finite values.
Results may differ from a plain program's by a relative error of at most 0.0003.
Values may be sent and summed in bfloat16 or wider, within the bound.
No kernel may reach another device: no remote copies, remote signals or barrier semaphores. Data moves between devices by JAX's collectives and lax.ppermute only.
A program may use at most 128 MiB of HBM per device.

v0:
```python
import math

import jax
import jax.numpy as jnp
from jax import lax
from jax.sharding import PartitionSpec as P


def mixing_matrix(weight_rows, axis):
    real_part = lax.index_in_dim(weight_rows, 0, axis, keepdims=False)
    imag_part = lax.index_in_dim(weight_rows, 1, axis, keepdims=False)
    upper = jnp.stack([real_part, -imag_part], axis=-2)
    lower = jnp.stack([imag_part, real_part], axis=-2)
    return jnp.stack([upper, lower], axis=axis)


def fourier_tables(extent):
    counter = jnp.arange(extent, dtype=jnp.int32)
    phase = counter[:, None] * counter[None, :] % extent
    angle = phase.astype(jnp.float32) * (2.0 * math.pi / extent)
    return (jnp.cos(angle), jnp.sin(angle))


def product(left, right):
    return jnp.matmul(left, right, precision=lax.Precision.HIGHEST)


def build_dedispersion(sweep_response_taps, chirp_length):
    longest = sweep_response_taps.shape[3]
    block_size = 2 * longest
    cosines, sines = fourier_tables(block_size)
    lag = jnp.arange(longest, dtype=jnp.int32)
    inside = lag[None, :] < chirp_length[:, None]
    factor = lax.rsqrt(chirp_length.astype(jnp.float32))[:, None]
    resp_real = jnp.where(inside, sweep_response_taps[0, 0], 0.0) * factor
    resp_imag = jnp.where(inside, sweep_response_taps[0, 1], 0.0) * factor
    freq_real = product(resp_real, cosines[:longest]) + product(resp_imag, sines[:longest])
    freq_imag = product(resp_imag, cosines[:longest]) - product(resp_real, sines[:longest])
    gain_real = freq_real[:, None, :]
    gain_imag = freq_imag[:, None, :]
    back_cos = cosines[:, longest:]
    back_sin = sines[:, longest:]

    def dedisperse(series):
        total = series.shape[3]
        count = total // longest
        padding = jnp.zeros(series.shape[:3] + (longest,), jnp.float32)
        padded = jnp.concatenate([padding, series], axis=3)
        front = padded[..., :total].reshape(series.shape[:3] + (count, longest))
        behind = padded[..., longest:].reshape(series.shape[:3] + (count, longest))
        blocks = jnp.concatenate([front, behind], axis=4)
        spec_real = product(blocks[0], cosines) + product(blocks[1], sines)
        spec_imag = product(blocks[1], cosines) - product(blocks[0], sines)
        prod_real = spec_real * gain_real - spec_imag * gain_imag
        prod_imag = spec_real * gain_imag + spec_imag * gain_real
        out_real = (product(prod_real, back_cos) - product(prod_imag, back_sin)) / block_size
        out_imag = (product(prod_imag, back_cos) + product(prod_real, back_sin)) / block_size
        return jnp.stack([out_real, out_imag], 0).reshape(series.shape)

    return dedisperse


def on_device(voltages, weights, channel_map, sweep_response_taps, chirp_length):
    selected = jnp.take(voltages, channel_map, axis=2)
    mixing = mixing_matrix(weights[0], 0)
    beams = jnp.einsum(
        "opbra,rpat->opbt",
        mixing,
        lax.all_to_all(selected, "chan", split_axis=2, concat_axis=3, tiled=True)[:, :, 0],
        preferred_element_type=jnp.float32,
    )
    dedisperse = build_dedispersion(sweep_response_taps, chirp_length)
    result = dedisperse(lax.all_to_all(beams, "tm", split_axis=2, concat_axis=3, tiled=True))
    return result[None]


def solution(mesh):
    return jax.shard_map(
        on_device,
        mesh=mesh,
        in_specs=(
            P(None, None, None, "chan", "tm"),
            P("chan", None, None, None, None),
            P(),
            P("chan", None, "tm", None),
            P("tm"),
        ),
        out_specs=P("chan", None, None, "tm", None),
        check_vma=False,
    )
```

profile of v0, /device:TPU:6, one launch (start us, length us, event | category | flops | bytes accessed | tf_op | source)
XLA Modules:
  0.0 261.1 jit_solution(3324275978289467517)
XLA Ops:
  0.0 0.7 compare_select_fusion
  0.7 0.7 compare_and_fusion
  1.3 8.9 %gather_fusion = bf16[64,2,2,32,512]{4,3,2,1,0:T(8,128)(2,1)} fusion(bf16[2,2,64,32,512]{4,3,2,1,0:T(8,128)(2,1)} %param.5, s32[1024]{0:T(1024)S(1)} %pad_clamp_fusion), kind=kCustom, calls=%fused_computation | custom fusion | bytes 16777472 | tf_op jit(solution)/shard_map/jit(_take)/gather | solution.py:64
  10.3 7.5 %select_bitcast_fusion = bf16[2,2,64,32,512]{4,3,1,0,2:T(8,128)(2,1)} fusion(bf16[64,2,2,32,512]{4,3,2,1,0:T(8,128)(2,1)} %gather_fusion, pred[64]{0:T(512)(128)(4,1)S(1)} %compare_and_fusion), kind=kLoop, calls=%fused_computation.1 | loop fusion | flops 4194304 | bytes 16777280 | tf_op jit(solution)/shard_map/jit(_take)/select_n | solution.py:64
  17.8 12.3 %all-to-all-start = ((bf16[2,2,64,32,512]{4,3,1,0,2:T(8,128)(2,1)}), bf16[2,2,64,32,512]{4,3,1,0,2:T(8,128)(2,1)}, u32[]{:S(2)}, u32[]{:S(2)}) async-start(bf16[2,2,64,32,512]{4,3,1,0,2:T(8,128)(2,1)} %select_bitcast_fusion), calls=%async_computation | async-start | bytes 16777216 | tf_op jit(solution)/shard_map/all_to_all | solution.py:69
  30.1 3.8 %fusion.18 = f32[512,512]{1,0:T(8,128)S(1)} fusion(), kind=kLoop, calls=%fused_computation.34 | loop fusion | flops 3670016 | bytes 1048576 | tf_op jit(solution)/shard_map/cos | solution.py:21
  33.8 3.8 %fusion.17 = f32[512,512]{1,0:T(8,128)S(1)} fusion(), kind=kLoop, calls=%fused_computation.33 | loop fusion | flops 3670016 | bytes 1048576 | tf_op jit(solution)/shard_map/sin | solution.py:21
  38.1 0.4 fusion.25
  38.4 0.4 convolution_add_fusion.2
  39.0 174.1 %all-to-all-done = bf16[2,2,64,32,512]{4,3,1,0,2:T(8,128)(2,1)} async-done(((bf16[2,2,64,32,512]{4,3,1,0,2:T(8,128)(2,1)}), bf16[2,2,64,32,512]{4,3,1,0,2:T(8,128)(2,1)}, u32[]{:S(2)}, u32[]{:S(2)}) %all-to-all-start) | async-done | bytes 8388640 | tf_op jit(solution)/shard_map/all_to_all | solution.py:69
  213.1 8.3 %copy.12 = bf16[2,2,64,32,512]{4,3,2,0,1:T(8,128)(2,1)} copy(bf16[2,2,64,32,512]{4,3,1,0,2:T(8,128)(2,1)} %all-to-all-done) | data formatting | bytes 16777216 | tf_op jit(solution)/shard_map/all_to_all | solution.py:69
  221.4 4.9 %convolution_bitcast_fusion = f32[2,2,32,512]{3,2,0,1:T(8,128)S(1)} fusion(bf16[2,2,2048,512,1]{3,2,0,4,1:T(8,128)(2,1)} %bitcast.84, bf16[1,2,32,2,2048]{4,2,3,0,1:T(8,128)(2,1)S(1)} %get-tuple-element.8, bf16[1,2,32,2,2048]{4,2,3,0,1:T(8,128)(2,1)S(1)} %get-tuple-element.7), kind=kOutput, calls=%fused_computation.7 | convolution fusion | flops 538968064 | bytes 9699328 | tf_op jit(solution)/shard_map/opbra,rpat->opbt/dot_general | solution.py:66
  226.3 0.9 copy.14
  227.2 4.5 %all-to-all-start.1 = ((f32[2,2,32,512]{3,0,1,2:T(2,128)}), f32[2,2,32,512]{3,0,1,2:T(2,128)S(1)}, u32[]{:S(2)}, u32[]{:S(2)}) async-start(f32[2,2,32,512]{3,0,1,2:T(2,128)} %copy.14), calls=%async_computation.1 | async-start | bytes 524288 | tf_op jit(solution)/shard_map/all_to_all | solution.py:73
  232.1 6.3 %all-to-all-done.1 = f32[2,2,32,512]{3,0,1,2:T(2,128)S(1)} async-done(((f32[2,2,32,512]{3,0,1,2:T(2,128)}), f32[2,2,32,512]{3,0,1,2:T(2,128)S(1)}, u32[]{:S(2)}, u32[]{:S(2)}) %all-to-all-start.1) | async-done | bytes 262176 | tf_op jit(solution)/shard_map/all_to_all | solution.py:73
  239.1 4.9 %fusion.12 = f32[2,8,8,512]{3,2,1,0:T(8,128)S(1)} fusion(f32[2,2,8,8,512]{4,3,2,1,0:T(8,128)S(1)} %constant_dynamic-update-slice_fusion), kind=kOutput, calls=%fused_computation.24 | convolution fusion | flops 406323200 | bytes 524288 | tf_op jit(solution)/shard_map/dot_general | solution.py:25
  243.9 4.9 %fusion.10 = f32[2,8,8,512]{3,2,1,0:T(8,128)S(1)} fusion(f32[2,2,8,8,512]{4,3,2,1,0:T(8,128)S(1)} %constant_dynamic-update-slice_fusion), kind=kOutput, calls=%fused_computation.22 | convolution fusion | flops 406323200 | bytes 524288 | tf_op jit(solution)/shard_map/dot_general | solution.py:25
  248.8 4.9 %convolution_add_fusion = f32[2,8,8,512]{3,2,1,0:T(8,128)S(1)} fusion(f32[2,8,8,512]{3,2,1,0:T(8,128)S(1)} %fusion.12, f32[2,2,8,8,512]{4,3,2,1,0:T(8,128)S(1)} %constant_dynamic-update-slice_fusion), kind=kOutput, calls=%fused_computation.6 | convolution fusion | flops 406388736 | bytes 786432 | tf_op jit(solution)/shard_map/dot_general | solution.py:25
  253.7 4.9 %convolution_subtract_fusion = f32[2,8,8,512]{3,2,1,0:T(8,128)S(1)} fusion(f32[2,8,8,512]{3,2,1,0:T(8,128)S(1)} %fusion.10, f32[2,2,8,8,512]{4,3,2,1,0:T(8,128)S(1)} %constant_dynamic-update-slice_fusion), kind=kOutput, calls=%fused_computation.5 | convolution fusion | flops 406388736 | bytes 786432 | tf_op jit(solution)/shard_map/dot_general | solution.py:25
  258.5 0.4 fusion.30
  259.0 0.4 fusion.29
  259.4 0.4 fusion.1
  259.9 0.4 fusion
  260.4 0.7 pad_maximum_fusion
  (22 shorter events, 1.6 us)
Async XLA Ops:
  17.7 19.9 %copy-start.2 = (s32[8]{0:T(128)S(1)}, s32[8]{0:T(128)}, u32[]{:S(2)}) copy-start(s32[8]{0:T(128)} %param.9) | copy-start | bytes 100
  17.7 19.9 %copy-start.1 = (f32[1,2,8,256]{3,2,1,0:T(8,128)S(1)}, f32[1,2,8,256]{3,2,1,0:T(8,128)}, u32[]{:S(2)}) copy-start(f32[1,2,8,256]{3,2,1,0:T(8,128)} %param.8) | copy-start | bytes 49156
  17.7 21.1 %copy-start = (bf16[1,2,2,32,2048]{4,3,2,1,0:T(8,128)(2,1)S(1)}, bf16[1,2,2,32,2048]{4,3,2,1,0:T(8,128)(2,1)}, u32[]{:S(2)}) copy-start(bf16[1,2,2,32,2048]{4,3,2,1,0:T(8,128)(2,1)} %param.6) | copy-start | bytes 1572868
  17.8 195.4 %all-to-all-start = ((bf16[2,2,64,32,512]{4,3,1,0,2:T(8,128)(2,1)}), bf16[2,2,64,32,512]{4,3,1,0,2:T(8,128)(2,1)}, u32[]{:S(2)}, u32[]{:S(2)}) async-start(bf16[2,2,64,32,512]{4,3,1,0,2:T(8,128)(2,1)} %select_bitcast_fusion), calls=%async_computation | async-start | bytes 16777216 | tf_op jit(solution)/shard_map/all_to_all | solution.py:69
  227.2 11.1 %all-to-all-start.1 = ((f32[2,2,32,512]{3,0,1,2:T(2,128)}), f32[2,2,32,512]{3,0,1,2:T(2,128)S(1)}, u32[]{:S(2)}, u32[]{:S(2)}) async-start(f32[2,2,32,512]{3,0,1,2:T(2,128)} %copy.14), calls=%async_computation.1 | async-start | bytes 524288 | tf_op jit(solution)/shard_map/all_to_all | solution.py:73
where the time goes:
time: 265 us; the launch traced here: 261 us
  waiting for transfers between devices  180 us (68%)
  matrix products  27.6 us (10%)
  local copies, waits for them, and re-layouts  18.8 us (7%)
  other arithmetic  17.2 us (6%)
  starting transfers between devices  16.8 us (6%)
    all_to_all x1, waiting for transfers between devices, on_device(): lax.all_to_all(selected, 'chan', split_axis=2, concat_axis=3, tiled=True)  174 us
    dot_general x12, matrix products, product(): return jnp.matmul(left, right, precision=lax.Precision.HIGHEST)  22.6 us
    all_to_all x1, starting transfers between devices, on_device(): lax.all_to_all(selected, 'chan', split_axis=2, concat_axis=3, tiled=True)  12.3 us
    gather x1, local copies, waits for them, and re-layouts, on_device(): selected = jnp.take(voltages, channel_map, axis=2)  8.93 us
    all_to_all x1, local copies, waits for them, and re-layouts, on_device(): lax.all_to_all(selected, 'chan', split_axis=2, concat_axis=3, tiled=True)  8.28 us
    select_n x2, other arithmetic, on_device(): selected = jnp.take(voltages, channel_map, axis=2)  8.14 us
    all_to_all x1, waiting for transfers between devices, on_device(): lax.all_to_all(beams, 'tm', split_axis=2, concat_axis=3, tiled=True)  6.32 us
  transfers between devices with their start and end apart: 2, of which 2 were waited for; matrix products, arithmetic and copies ran while one was open for 4% of the time, Pallas kernels for 0%

commit v1 on v0

--- a/solution.py
+++ b/solution.py
@@ -62,13 +62,15 @@
 
 def on_device(voltages, weights, channel_map, sweep_response_taps, chirp_length):
     selected = jnp.take(voltages, channel_map, axis=2)
-    mixing = mixing_matrix(weights[0], 0)
-    beams = jnp.einsum(
-        "opbra,rpat->opbt",
+    local_weights = lax.all_to_all(weights, "chan", split_axis=4, concat_axis=0, tiled=True)
+    mixing = mixing_matrix(local_weights, 1)
+    partial = jnp.einsum(
+        "jopbra,rpjat->jopbt",
         mixing,
-        lax.all_to_all(selected, "chan", split_axis=2, concat_axis=3, tiled=True)[:, :, 0],
+        selected,
         preferred_element_type=jnp.float32,
     )
+    beams = lax.psum_scatter(partial, "chan", scatter_dimension=0, tiled=True)[0]
     dedisperse = build_dedispersion(sweep_response_taps, chirp_length)
     result = dedisperse(lax.all_to_all(beams, "tm", split_axis=2, concat_axis=3, tiled=True))
     return result[None]

time: 265 us -> 290 us (1.094)
  between operations: 0.21 us -> 13.6 us
  waiting for transfers between devices: 180 us -> 192 us
  other arithmetic: 17.2 us -> 9.3 us
  local copies, waits for them, and re-layouts: 18.8 us -> 25.7 us
  matrix products: 27.6 us -> 32 us
    unnamed x0 -> x2, waiting for transfers between devices: none -> 177 us
    all_to_all x1, waiting for transfers between devices: 174 us -> 8.54 us  [on_device(): lax.all_to_all(weights, 'chan', split_axis=4, concat_axis=0, tiled=True)]
    unnamed x8 -> x11, local copies, waits for them, and re-layouts: 0.12 us -> 9.17 us
    select_n x2 -> x1, other arithmetic: 8.14 us -> 0.01 us  [on_device(): selected = jnp.take(voltages, channel_map, axis=2)]
    dot_general x1, matrix products: 4.94 us -> 9.35 us  [on_device(): jnp.einsum('jopbra,rpjat->jopbt', mixing, selected, preferred_element_typ...]
    all_to_all x1, local copies, waits for them, and re-layouts: 8.28 us -> 4.75 us  [on_device(): lax.all_to_all(weights, 'chan', split_axis=4, concat_axis=0, tiled=True)]
  transfers between devices with their start and end apart: 2 -> 3, of which waited for: 2 -> 3; matrix products, arithmetic and copies ran while one was open for 4% -> 6% of each run, Pallas kernels for 0% -> 0%
where the time goes in v1:
time: 290 us; the launch traced here: 289 us
  waiting for transfers between devices  192 us (66%)
  matrix products  32 us (11%)
  local copies, waits for them, and re-layouts  25.7 us (9%)
  starting transfers between devices  16.3 us (6%)
  between operations  13.6 us (5%)
  other arithmetic  9.3 us (3%)
    unnamed x2, waiting for transfers between devices  177 us
    dot_general x12, matrix products, product(): return jnp.matmul(left, right, precision=lax.Precision.HIGHEST)  22.6 us
    all_to_all x1, starting transfers between devices, on_device(): lax.all_to_all(weights, 'chan', split_axis=4, concat_axis=0, tiled=True)  12 us
    dot_general x1, matrix products, on_device(): jnp.einsum('jopbra,rpjat->jopbt', mixing, selected, preferred_element_typ...  9.35 us
    unnamed x11, local copies, waits for them, and re-layouts  9.17 us
    gather x1, local copies, waits for them, and re-layouts, on_device(): selected = jnp.take(voltages, channel_map, axis=2)  8.92 us
    all_to_all x1, waiting for transfers between devices, on_device(): lax.all_to_all(weights, 'chan', split_axis=4, concat_axis=0, tiled=True)  8.54 us
    all_to_all x1, waiting for transfers between devices, on_device(): lax.all_to_all(beams, 'tm', split_axis=2, concat_axis=3, tiled=True)  6.32 us
  transfers between devices with their start and end apart: 3, of which 3 were waited for; matrix products, arithmetic and copies ran while one was open for 6% of the time, Pallas kernels for 0%

profile of v1, /device:TPU:6, one launch (start us, length us, event | category | flops | bytes accessed | tf_op | source)
XLA Modules:
  0.0 288.9 jit_solution(12789684402102642701)
XLA Ops:
  6.5 4.3 %copy.13 = bf16[1,2,2,32,2048]{3,2,1,0,4:T(2,128)(2,1)S(1)} copy(bf16[1,2,2,32,2048]{4,3,2,1,0:T(8,128)(2,1)} %param.6) | data formatting | bytes 1048576 | tf_op args[1]
  10.8 2.8 reshape.48
  13.6 12.0 %all-to-all-start = ((bf16[64,2,2048]{2,1,0:T(2,128)(2,1)}), bf16[64,2,2048]{2,1,0:T(2,128)(2,1)S(1)}, u32[]{:S(2)}, u32[]{:S(2)}) async-start(bf16[64,2,2048]{2,1,0:T(2,128)(2,1)} %reshape.48), calls=%async_computation | async-start | bytes 1048576 | tf_op jit(solution)/shard_map/all_to_all | solution.py:65
  25.6 8.9 %gather_fusion = bf16[64,2,2,32,512]{4,3,2,1,0:T(8,128)(2,1)} fusion(bf16[2,2,64,32,512]{4,3,2,1,0:T(8,128)(2,1)} %param.5, s32[1024]{0:T(1024)S(1)} %pad_clamp_fusion), kind=kCustom, calls=%fused_computation | custom fusion | bytes 16777472 | tf_op jit(solution)/shard_map/jit(_take)/gather | solution.py:64
  34.5 8.5 %all-to-all-done = bf16[64,2,2048]{2,1,0:T(2,128)(2,1)S(1)} async-done(((bf16[64,2,2048]{2,1,0:T(2,128)(2,1)}), bf16[64,2,2048]{2,1,0:T(2,128)(2,1)S(1)}, u32[]{:S(2)}, u32[]{:S(2)}) %all-to-all-start) | async-done | bytes 524320 | tf_op jit(solution)/shard_map/all_to_all | solution.py:65
  43.1 2.0 reshape.49
  45.1 4.7 %copy.15 = bf16[1,2,2,32,64,32]{5,3,2,4,1,0:T(8,128)(2,1)S(1)} copy(bf16[1,2,2,32,64,32]{3,2,1,5,4,0:T(2,128)(2,1)} %bitcast.93) | data formatting | bytes 1048576 | tf_op jit(solution)/shard_map/all_to_all | solution.py:65
  50.4 0.8 maximum_bitcast_fusion
  51.3 9.3 %convolution_bitcast_fusion = f32[64,2,2,32,512]{4,3,1,2,0:T(8,128)} fusion(bf16[64,1,2,32,2,32]{5,3,4,1,2,0:T(8,128)(2,1)S(1)} %get-tuple-element.8, bf16[64,1,2,32,2,32]{5,3,4,1,2,0:T(8,128)(2,1)S(1)} %get-tuple-element.7, bf16[64,2,2,32,512]{4,3,2,1,0:T(8,128)(2,1)} %gather_fusion, pred[64]{0:T(512)(128)(4,1)S(1)} %compare_and_fusion), kind=kOutput, calls=%fused_computation.1 | convolution fusion | flops 543162368 | bytes 26214464 | tf_op jit(solution)/shard_map/jopbra,rpjat->jopbt/dot_general | solution.py:67
  60.6 3.8 %fusion.19 = f32[512,512]{1,0:T(8,128)S(1)} fusion(), kind=kLoop, calls=%fused_computation.37 | loop fusion | flops 3670016 | bytes 1048576 | tf_op jit(solution)/shard_map/cos | solution.py:21
  64.4 3.8 %fusion.18 = f32[512,512]{1,0:T(8,128)S(1)} fusion(), kind=kLoop, calls=%fused_computation.36 | loop fusion | flops 3670016 | bytes 1048576 | tf_op jit(solution)/shard_map/sin | solution.py:21
  69.4 177.2 %reduce-scatter.4.cloned.1.call-done = f32[1,2,2,32,512]{4,3,1,2,0:T(8,128)} async-done(((f32[64,2,2,32,512]{4,3,1,2,0:T(8,128)}), f32[1,2,2,32,512]{4,3,1,2,0:T(8,128)}) %reduce-scatter.4.cloned.1.call-update) | async-done | bytes 262160
  246.6 1.9 copy.18
  248.5 4.3 %all-to-all-start.1 = ((f32[2,2,32,512]{3,0,1,2:T(2,128)}), f32[2,2,32,512]{3,0,1,2:T(2,128)S(1)}, u32[]{:S(2)}, u32[]{:S(2)}) async-start(f32[2,2,32,512]{3,0,1,2:T(2,128)} %copy.18), calls=%async_computation.1 | async-start | bytes 524288 | tf_op jit(solution)/shard_map/all_to_all | solution.py:75
  253.1 6.3 %all-to-all-done.1 = f32[2,2,32,512]{3,0,1,2:T(2,128)S(1)} async-done(((f32[2,2,32,512]{3,0,1,2:T(2,128)}), f32[2,2,32,512]{3,0,1,2:T(2,128)S(1)}, u32[]{:S(2)}, u32[]{:S(2)}) %all-to-all-start.1) | async-done | bytes 262176 | tf_op jit(solution)/shard_map/all_to_all | solution.py:75
  260.1 4.9 %fusion.13 = f32[2,8,8,512]{3,2,1,0:T(8,128)S(1)} fusion(f32[2,2,8,8,512]{4,3,2,1,0:T(8,128)S(1)} %constant_dynamic-update-slice_fusion), kind=kOutput, calls=%fused_computation.29 | convolution fusion | flops 406323200 | bytes 524288 | tf_op jit(solution)/shard_map/dot_general | solution.py:25
  264.9 4.9 %fusion.11 = f32[2,8,8,512]{3,2,1,0:T(8,128)S(1)} fusion(f32[2,2,8,8,512]{4,3,2,1,0:T(8,128)S(1)} %constant_dynamic-update-slice_fusion), kind=kOutput, calls=%fused_computation.27 | convolution fusion | flops 406323200 | bytes 524288 | tf_op jit(solution)/shard_map/dot_general | solution.py:25
  269.8 4.9 %convolution_add_fusion = f32[2,8,8,512]{3,2,1,0:T(8,128)S(1)} fusion(f32[2,8,8,512]{3,2,1,0:T(8,128)S(1)} %fusion.13, f32[2,2,8,8,512]{4,3,2,1,0:T(8,128)S(1)} %constant_dynamic-update-slice_fusion), kind=kOutput, calls=%fused_computation.13 | convolution fusion | flops 406388736 | bytes 786432 | tf_op jit(solution)/shard_map/dot_general | solution.py:25
  274.7 4.9 %convolution_subtract_fusion = f32[2,8,8,512]{3,2,1,0:T(8,128)S(1)} fusion(f32[2,8,8,512]{3,2,1,0:T(8,128)S(1)} %fusion.11, f32[2,2,8,8,512]{4,3,2,1,0:T(8,128)S(1)} %constant_dynamic-update-slice_fusion), kind=kOutput, calls=%fused_computation.12 | convolution fusion | flops 406388736 | bytes 786432 | tf_op jit(solution)/shard_map/dot_general | solution.py:25
  279.6 0.4 fusion.31
  280.0 0.4 fusion.30
  280.4 0.4 fusion.5
  280.9 0.4 fusion.4
  281.4 0.7 pad_maximum_fusion
  (27 shorter events, 2.8 us)
Async XLA Ops:
  6.5 19.0 %copy-start.2 = (s32[64]{0:T(128)S(1)}, s32[64]{0:T(128)}, u32[]{:S(2)}) copy-start(s32[64]{0:T(128)} %param.7) | copy-start | bytes 772
  13.6 29.5 %all-to-all-start = ((bf16[64,2,2048]{2,1,0:T(2,128)(2,1)}), bf16[64,2,2048]{2,1,0:T(2,128)(2,1)S(1)}, u32[]{:S(2)}, u32[]{:S(2)}) async-start(bf16[64,2,2048]{2,1,0:T(2,128)(2,1)} %reshape.48), calls=%async_computation | async-start | bytes 1048576 | tf_op jit(solution)/shard_map/all_to_all | solution.py:65
  25.5 221.1 %reduce-scatter.4.cloned.1.call-start = ((), (), s32[]{:S(2)}) async-start(), calls=%async_computation.3 | async-start | bytes 17039360
  60.6 7.6 %copy-start.1 = (s32[8]{0:T(128)S(1)}, s32[8]{0:T(128)}, u32[]{:S(2)}) copy-start(s32[8]{0:T(128)} %param.9) | copy-start | bytes 100
  60.6 7.7 %copy-start = (f32[1,2,8,256]{3,2,1,0:T(8,128)S(1)}, f32[1,2,8,256]{3,2,1,0:T(8,128)}, u32[]{:S(2)}) copy-start(f32[1,2,8,256]{3,2,1,0:T(8,128)} %param.8) | copy-start | bytes 49156
  248.5 10.9 %all-to-all-start.1 = ((f32[2,2,32,512]{3,0,1,2:T(2,128)}), f32[2,2,32,512]{3,0,1,2:T(2,128)S(1)}, u32[]{:S(2)}, u32[]{:S(2)}) async-start(f32[2,2,32,512]{3,0,1,2:T(2,128)} %copy.18), calls=%async_computation.1 | async-start | bytes 524288 | tf_op jit(solution)/shard_map/all_to_all | solution.py:75
Sparse Core Ops, SparseCore 0:
  60.8 185.7 reduce-scatter.3
